TPU v7x, 256 devices: a whole 4x4x8 slice. The times are simulated.
256 devices in a mesh: blk: 32 (over x, y, core), row: 8 (over z).
Axes of the slice: x: 4, y: 4, z: 8, core: 2. Of those that a mesh axis runs over, the one named last changes fastest.
Arguments:
- samples: bfloat16 [1024, 8192], P('blk', 'row'), may hold values from -8 to 8, as said below
- blocks: int32 [64, 4], replicated, may hold values from 0 to 31
- factor: float32 [64, 1024], P(None, 'row'), may hold values from -1.2 to 1.2
Outputs:
- cumulants: float32 [64, 1024, 1024], P('blk', 'row')
- factor_out: float32 [64, 1024], P(None, 'row')
Inputs may be any that keep to these rules, and one draw needn't show every extreme that they name: `samples`: channel values are drawn with mean zero.
All inputs are finite; a program needn't handle non-finite values.
Results may differ from a plain program's by a relative error of at most 0.0014.
Values may be sent and summed in bfloat16 or wider, within the bound.
No kernel may reach another device: no remote copies, remote signals or barrier semaphores. Data moves between devices by JAX's collectives and lax.ppermute only.
A program may use at most 64 MiB of HBM per device.

v0:
```python
import jax
import jax.numpy as jnp
from jax import lax
from jax.sharding import PartitionSpec as P

CHANNELS = 1024
BLOCK = 32
RANK = 64
SAMPLES = 8192
ITERS = 2
step_size = 0.2


def pair_rows(left, right):
    product = left[:, None, :].astype(jnp.float32) * right[None, :, :].astype(jnp.float32)
    return product.reshape(left.shape[0] * right.shape[0], left.shape[1]).astype(jnp.bfloat16)


def contract_last(left, right):
    return lax.dot_general(
        left, right, (((1,), (1,)), ((), ())), preferred_element_type=jnp.float32
    )


def gauss_terms(gram, count, width, row_lo):
    highest = lax.Precision.HIGHEST

    def part(first, second):
        return gram[first * width : (first + 1) * width, second * width : (second + 1) * width]

    cov_ab = lax.dynamic_slice_in_dim(part(0, 1), row_lo, count, 0)
    cov_ac = lax.dynamic_slice_in_dim(part(0, 2), row_lo, count, 0)
    cov_ad = lax.dynamic_slice_in_dim(part(0, 3), row_lo, count, 0)
    cov_cd = part(2, 3)
    cov_bd = part(1, 3)
    cov_bc = part(1, 2)
    first_term = cov_ab.reshape(-1)[:, None] * cov_cd.reshape(-1)[None, :]
    second_term = jnp.einsum("ik,jl->ijkl", cov_ac, cov_bd, precision=highest).reshape(
        count * width, width * width
    )
    third_term = jnp.einsum("il,jk->ijkl", cov_ad, cov_bc, precision=highest).reshape(
        count * width, width * width
    )
    return first_term + second_term + third_term


def add_cols(total, piece, start):
    old = lax.dynamic_slice_in_dim(total, start, piece.shape[1], 1)
    return lax.dynamic_update_slice_in_dim(total, old + piece, start, 1)


def add_grads(total, kslab, full, ids, row_lo, count, width):
    highest = lax.Precision.HIGHEST
    rank = full.shape[0]
    start_a = ids[0] * width + row_lo
    fac_a = lax.dynamic_slice_in_dim(full, start_a, count, 1)
    fac_b = lax.dynamic_slice_in_dim(full, ids[1] * width, width, 1)
    fac_c = lax.dynamic_slice_in_dim(full, ids[2] * width, width, 1)
    fac_d = lax.dynamic_slice_in_dim(full, ids[3] * width, width, 1)
    upair = (fac_a[:, :, None] * fac_b[:, None, :]).reshape(rank, count * width)
    vpair = (fac_c[:, :, None] * fac_d[:, None, :]).reshape(rank, width * width)
    model = lax.dot_general(upair, vpair, (((0,), (0,)), ((), ())), precision=highest)
    resid = kslab - model
    wmat = lax.dot_general(vpair, resid, (((1,), (1,)), ((), ())), precision=highest).reshape(
        rank, count, width
    )
    zmat = jnp.dot(upair, resid, precision=highest).reshape(rank, width, width)
    total = add_cols(total, jnp.sum(wmat * fac_b[:, None, :], axis=2), start_a)
    total = add_cols(total, jnp.sum(wmat * fac_a[:, :, None], axis=1), ids[1] * width)
    total = add_cols(total, jnp.sum(zmat * fac_d[:, None, :], axis=2), ids[2] * width)
    total = add_cols(total, jnp.sum(zmat * fac_c[:, :, None], axis=1), ids[3] * width)
    return total


def gather_factor(columns):
    return lax.all_gather(columns, "row", axis=1, tiled=True)


def per_device(samples, blocks, factor):
    width = BLOCK
    row_count = lax.axis_size("row")
    count = width // row_count
    row_lo = lax.axis_index("row") * count
    per_owner = blocks.shape[0] // lax.axis_size("blk")
    mine = lax.dynamic_slice_in_dim(blocks, lax.axis_index("blk") * per_owner, per_owner, 0)
    needed = mine.reshape(-1)
    pairs = width * width
    piece = lax.all_gather(samples, "blk", axis=0, tiled=True)
    pieces = piece.shape[0] // width
    owned = jnp.arange(pieces, dtype=jnp.int32)
    select = (needed[:, None] == owned[None, :]).astype(jnp.bfloat16)
    shaped = piece.reshape(pieces, width, piece.shape[1])
    taken = jnp.einsum("mb,bcs->mcs", select, shaped, preferred_element_type=jnp.float32)
    local = taken.astype(jnp.bfloat16)
    slabs = []
    whole = lax.all_gather(local, "row", axis=2, tiled=True)
    sample_block = min(SAMPLES, 2048)
    for slot in range(per_owner):
        source_a = whole[4 * slot]
        source_b = whole[4 * slot + 1]
        source_c = whole[4 * slot + 2]
        source_d = whole[4 * slot + 3]

        def accumulate(index, moment):
            low = index * sample_block
            left = lax.dynamic_slice(source_a, (row_lo, low), (count, sample_block))
            right = lax.dynamic_slice_in_dim(source_b, low, sample_block, 1)
            third = lax.dynamic_slice_in_dim(source_c, low, sample_block, 1)
            fourth = lax.dynamic_slice_in_dim(source_d, low, sample_block, 1)
            pmat = pair_rows(left, right)
            qmat = pair_rows(third, fourth)
            return moment + contract_last(pmat, qmat)

        moment = lax.fori_loop(
            0, SAMPLES // sample_block, accumulate, jnp.zeros((count * width, pairs), jnp.float32)
        )
        moment = moment / SAMPLES
        joined = whole[4 * slot : 4 * slot + 4].reshape(4 * width, whole.shape[2])
        gram = contract_last(joined, joined) / SAMPLES
        slabs.append(moment - gauss_terms(gram, count, width, row_lo))
    columns = factor
    full = gather_factor(columns)
    for step in range(ITERS):
        grad = jnp.zeros(full.shape, jnp.float32)
        for slot in range(per_owner):
            grad = add_grads(grad, slabs[slot], full, mine[slot], row_lo, count, width)
        owned_cols = lax.psum_scatter(grad, "row", scatter_dimension=1, tiled=True)
        owned_cols = lax.psum(owned_cols, "blk")
        squares = lax.psum(jnp.sum(owned_cols * owned_cols), "row")
        scale = lax.rsqrt(squares / (RANK * CHANNELS) + 1e-06)
        columns = columns + step_size * scale * owned_cols
        if step + 1 < ITERS:
            full = gather_factor(columns)
    return (jnp.stack(slabs), columns)


def solution(mesh):
    placed = (P("blk", "row"), P(), P(None, "row"))
    return jax.shard_map(
        per_device,
        mesh=mesh,
        in_specs=placed,
        out_specs=(P("blk", "row", None), P(None, "row")),
        check_vma=False,
    )
```

profile of v0, /device:TPU:32, one launch (start us, length us, event | category | flops | bytes accessed | tf_op | source)
XLA Modules:
  0.0 646.9 jit_solution(17991353607669108797)
XLA Ops:
  8.2 53.5 %all-gather.3.cloned.1.call-done = bf16[1024,1024]{1,0:T(8,128)(2,1)} async-done(((bf16[32,1024]{1,0:T(8,128)(2,1)}), bf16[1024,1024]{1,0:T(8,128)(2,1)}) %all-gather.3.cloned.1.call-update) | async-done | bytes 2097168 | tf_op jit(solution)/shard_map/all_gather | solution.py:88
  61.8 4.7 fusion.2
  72.3 26.5 %all_gather.14 = f32[64,1024]{1,0:T(8,128)S(1)} all-gather(f32[64,128]{1,0:T(8,128)S(1)} %copy-done.11), channel_id=1, replica_groups=mesh['blk'=32,'row'=8] {'row'}, dimensions={1}, use_global_device_ids=true | all-gather | bytes 294912 | tf_op jit(solution)/shard_map/all_gather | solution.py:76
  101.3 19.8 %all-gather.5.cloned.1.call-done = bf16[8,32,8192]{2,0,1:T(8,128)(2,1)} async-done(((bf16[8,32,1024]{2,0,1:T(8,128)(2,1)}), bf16[8,32,8192]{2,0,1:T(8,128)(2,1)}) %all-gather.5.cloned.1.call-update) | async-done | bytes 4194320 | tf_op jit(solution)/shard_map/all_gather | solution.py:96
  121.1 21.7 %fusion.10 = (bf16[1,32,8192]{2,0,1:T(2,128)(2,1)S(1)}, bf16[1,32,8192]{2,0,1:T(2,128)(2,1)}, bf16[1,32,8192]{2,0,1:T(2,128)(2,1)}, bf16[1,32,8192]{2,0,1:T(2,12...) fusion(bf16[8,32,8192]{2,0,1:T(8,128)(2,1)} %all-gather.5.clone, ...), kind=kLoop, calls=%fused_computation.112 | loop fusion | bytes 8388608 | tf_op jit(solution)/shard_map/slice | solution.py:102
  145.9 31.4 %while.32 = (s32[]{:T(128)}, f32[128,1024]{1,0:T(8,128)S(1)}, bf16[32,8192]{1,0:T(8,128)(2,1)}, s32[]{:T(128)}, bf16[32,8192]{1,0:T(8,128)(2,1)S(1)}, /*index=5*...) while((s32[]{:T(128)}, f32[128,1024]{1,0:T(8,128)S(1)}, ...), condition=%wide.region_1.0_spmd.clone, body=%wide.region_0.0_spmd.clone.sunk | while | flops 542056448 | bytes 12533941 | solution.py:114
  146.0 3.0 multiply_convert_fusion.9
  150.0 3.8 convolution_add_fusion.4
  153.9 3.0 multiply_convert_fusion.9
  157.9 3.8 convolution_add_fusion.4
  161.7 3.0 multiply_convert_fusion.9
  165.7 3.8 convolution_add_fusion.4
  169.6 3.0 multiply_convert_fusion.9
  173.6 3.8 convolution_add_fusion.4
  177.4 6.7 %fusion.11 = (bf16[4,32,8192]{2,0,1:T(4,128)(2,1)S(1)}, bf16[4,32,8192]{2,0,1:T(4,128)(2,1)}) fusion(bf16[8,32,8192]{2,0,1:T(8,128)(2,1)} %all-gather.5.cloned.1.call-done), kind=kLoop, calls=%fused_computation.113 | loop fusion | bytes 8388608 | tf_op jit(solution)/shard_map/slice | solution.py:118
  197.6 3.6 copy_bitcast_fusion.2
  203.3 35.3 %while.33 = (s32[]{:T(128)}, f32[128,1024]{1,0:T(8,128)S(1)}, bf16[32,8192]{1,0:T(8,128)(2,1)}, s32[]{:T(128)}, bf16[32,8192]{1,0:T(8,128)(2,1)S(1)}, /*index=5*...) while((s32[]{:T(128)}, f32[128,1024]{1,0:T(8,128)S(1)}, ...), condition=%wide.region_3.0_spmd.clone, body=%wide.region_2.0_spmd.clone.sunk | while | flops 542056448 | bytes 12533941 | solution.py:114
  204.3 3.0 multiply_convert_fusion.11
  208.2 3.8 convolution_add_fusion.5
  213.0 3.0 multiply_convert_fusion.11
  217.0 3.8 convolution_add_fusion.5
  221.8 3.0 multiply_convert_fusion.11
  225.8 3.8 convolution_add_fusion.5
  230.6 3.0 multiply_convert_fusion.11
  234.6 3.8 convolution_add_fusion.5
  250.8 37.1 %reduce-scatter.3.cloned.1.call-done = f32[64,128]{0,1:T(8,128)} async-done(((f32[64,1024]{0,1:T(8,128)}), f32[64,128]{0,1:T(8,128)}) %reduce-scatter.3.cloned.1.call-update) | async-done | bytes 32784 | tf_op jit(solution)/shard_map/reduce_scatter | solution.py:127
  287.9 124.3 %psum.28 = f32[64,128]{0,1:T(8,128)S(1)} all-reduce(f32[64,128]{0,1:T(8,128)} %reduce-scatter.3.cloned.1.call-done), channel_id=1, replica_groups=mesh['blk'=32,'row'=8] {'blk'}, use_global_device_ids=true, to_apply=%region_13.0 | all-reduce | flops 8192 | bytes 65536 | tf_op jit(solution)/shard_map/psum | solution.py:128
  412.9 16.0 %psum.29 = f32[]{:T(128)} all-reduce(f32[]{:T(128)} %multiply_reduce_fusion.13), channel_id=1, replica_groups=mesh['blk'=32,'row'=8] {'row'}, use_global_device_ids=true, to_apply=%region_15.0 | all-reduce | flops 1 | bytes 8 | tf_op jit(solution)/shard_map/psum | solution.py:129
  429.7 24.3 %all_gather.15 = f32[64,1024]{0,1:T(8,128)S(1)} all-gather(f32[64,128]{0,1:T(8,128)S(1)} %multiply_add_fusion.1), channel_id=1, replica_groups=mesh['blk'=32,'row'=8] {'row'}, dimensions={1}, use_global_device_ids=true | all-gather | bytes 294912 | tf_op jit(solution)/shard_map/all_gather | solution.py:76
  463.1 34.0 %reduce-scatter.5.cloned.1.call-done = f32[64,128]{0,1:T(8,128)} async-done(((f32[64,1024]{0,1:T(8,128)}), f32[64,128]{0,1:T(8,128)}) %reduce-scatter.5.cloned.1.call-update) | async-done | bytes 32784 | tf_op jit(solution)/shard_map/reduce_scatter | solution.py:127
  497.1 124.3 %psum.30 = f32[64,128]{0,1:T(8,128)S(1)} all-reduce(f32[64,128]{0,1:T(8,128)} %reduce-scatter.5.cloned.1.call-done), channel_id=1, replica_groups=mesh['blk'=32,'row'=8] {'blk'}, use_global_device_ids=true, to_apply=%region_25.0 | all-reduce | flops 8192 | bytes 65536 | tf_op jit(solution)/shard_map/psum | solution.py:128
  623.1 15.9 %psum.31 = f32[]{:T(128)} all-reduce(f32[]{:T(128)} %multiply_reduce_fusion.8), channel_id=1, replica_groups=mesh['blk'=32,'row'=8] {'row'}, use_global_device_ids=true, to_apply=%region_27.0 | all-reduce | flops 1 | bytes 8 | tf_op jit(solution)/shard_map/psum | solution.py:129
  (159 shorter events, 58.7 us)
Async XLA Ops:
  7.2 0.8 copy-start
  7.2 65.1 %copy-start.11 = (f32[64,128]{1,0:T(8,128)S(1)}, f32[64,128]{1,0:T(8,128)}, u32[]{:S(2)}) copy-start(f32[64,128]{1,0:T(8,128)} %param.9) | copy-start | bytes 98308
  7.2 54.6 %all-gather.3.cloned.1.call-start = ((), (), s32[]{:S(2)}) async-start(), calls=%async_computation.2 | async-start | bytes 2162688 | tf_op jit(solution)/shard_map/all_gather | solution.py:88
  7.9 113.2 %all-gather.5.cloned.1.call-start = ((), (), s32[]{:S(2)}) async-start(), calls=%async_computation.3 | async-start | bytes 4718592 | tf_op jit(solution)/shard_map/all_gather | solution.py:96
  66.5 221.4 %reduce-scatter.3.cloned.1.call-start = ((), (), s32[]{:S(2)}) async-start(), calls=%async_computation.4 | async-start | bytes 589824 | tf_op jit(solution)/shard_map/reduce_scatter | solution.py:127
  192.3 2.1 copy-start.12
  194.4 1.5 copy-start.2
  196.5 4.6 copy-start.4
  196.5 4.6 copy-start.6
  197.6 3.6 copy-start.7
  242.8 1.5 copy-start.1
  244.3 3.4 copy-start.3
  244.3 3.4 copy-start.5
  245.9 3.3 copy-start.10
  249.9 0.8 copy-start.9
  250.7 246.3 %reduce-scatter.5.cloned.1.call-start = ((), (), s32[]{:S(2)}) async-start(), calls=%async_computation.5 | async-start | bytes 589824 | tf_op jit(solution)/shard_map/reduce_scatter | solution.py:127
  462.3 0.8 copy-start.8
Sparse Core Ops, SparseCore 0:
  10.6 51.1 all-gather.2
  66.6 54.4 all-gather.4
  250.8 36.9 reduce-scatter.2
  463.2 33.8 reduce-scatter.4
where the time goes:
time: 648 us; the launch traced here: 647 us
  blocking collectives  331 us (51%)
  waiting for transfers between devices  145 us (22%)
  local copies, waits for them, and re-layouts  57.5 us (9%)
  matrix products  47.2 us (7%)
  other arithmetic  44.2 us (7%)
  between operations  20.7 us (3%)
    psum x2, blocking collectives, per_device(): owned_cols = lax.psum(owned_cols, 'blk')  249 us
    reduce_scatter x2, waiting for transfers between devices, per_device(): owned_cols = lax.psum_scatter(grad, 'row', scatter_dimension=1, tiled=True)  71.1 us
    all_gather x1, waiting for transfers between devices, per_device(): piece = lax.all_gather(samples, 'blk', axis=0, tiled=True)  53.5 us
    all_gather x2, blocking collectives, gather_factor(): return lax.all_gather(columns, 'row', axis=1, tiled=True)  50.7 us
    psum x2, blocking collectives, per_device(): squares = lax.psum(jnp.sum(owned_cols * owned_cols), 'row')  32 us
    dot_general x10, matrix products, contract_last(): lax.dot_general(left, right, (((1,), (1,)), ((), ())), preferred_element_...  31.6 us
    convert_element_type x16, other arithmetic, pair_rows(): product.reshape(left.shape[0] * right.shape[0], left.shape[1])  24.8 us
    slice x1, local copies, waits for them, and re-layouts, per_device(): source_d = whole[4 * slot + 3]  21.7 us
  transfers between devices with their start and end apart: 4, of which 4 were waited for; matrix products, arithmetic and copies ran while one was open for 1% of the time, Pallas kernels for 0%

commit v1 on v0

--- a/solution.py
+++ b/solution.py
@@ -85,7 +85,13 @@
     mine = lax.dynamic_slice_in_dim(blocks, lax.axis_index("blk") * per_owner, per_owner, 0)
     needed = mine.reshape(-1)
     pairs = width * width
-    piece = lax.all_gather(samples, "blk", axis=0, tiled=True)
+
+    def start_masks(s0, a_name):
+        return jnp.concatenate(
+            lax.all_to_all(jnp.stack(lax.axis_size(a_name) * [s0]), a_name, 0, 0), axis=0
+        )
+
+    piece = start_masks(samples, "blk")
     pieces = piece.shape[0] // width
     owned = jnp.arange(pieces, dtype=jnp.int32)
     select = (needed[:, None] == owned[None, :]).astype(jnp.bfloat16)

time: 648 us -> 630 us (0.972)
  waiting for transfers between devices: 145 us -> 116 us
  starting transfers between devices: 0.16 us -> 7.44 us
    all_gather x1 -> x0, waiting for transfers between devices: 53.5 us -> none  [per_device(): piece = lax.all_gather(samples, 'blk', axis=0, tiled=True)]
    all_to_all x0 -> x1, waiting for transfers between devices: none -> 28.6 us  [start_masks(): lax.all_to_all(jnp.stack(lax.axis_size(a_name) * [s0]), a_name, 0, 0)]
    all_to_all x0 -> x1, starting transfers between devices: none -> 7.32 us  [start_masks(): lax.all_to_all(jnp.stack(lax.axis_size(a_name) * [s0]), a_name, 0, 0)]
where the time goes in v1:
time: 630 us; the launch traced here: 628 us
  blocking collectives  334 us (53%)
  waiting for transfers between devices  116 us (18%)
  local copies, waits for them, and re-layouts  60 us (10%)
  matrix products  45.6 us (7%)
  other arithmetic  44.2 us (7%)
  between operations  20.7 us (3%)
  starting transfers between devices  7.44 us (1%)
    psum x2, blocking collectives, per_device(): owned_cols = lax.psum(owned_cols, 'blk')  249 us
    reduce_scatter x2, waiting for transfers between devices, per_device(): owned_cols = lax.psum_scatter(grad, 'row', scatter_dimension=1, tiled=True)  70.8 us
    all_gather x2, blocking collectives, gather_factor(): return lax.all_gather(columns, 'row', axis=1, tiled=True)  52.9 us
    psum x2, blocking collectives, per_device(): squares = lax.psum(jnp.sum(owned_cols * owned_cols), 'row')  32 us
    dot_general x10, matrix products, contract_last(): lax.dot_general(left, right, (((1,), (1,)), ((), ())), preferred_element_...  31.6 us
    all_to_all x1, waiting for transfers between devices, start_masks(): lax.all_to_all(jnp.stack(lax.axis_size(a_name) * [s0]), a_name, 0, 0)  28.6 us
    convert_element_type x16, other arithmetic, pair_rows(): product.reshape(left.shape[0] * right.shape[0], left.shape[1])  24.8 us
    slice x1, local copies, waits for them, and re-layouts, per_device(): source_d = whole[4 * slot + 3]  21.7 us
  transfers between devices with their start and end apart: 4, of which 4 were waited for; matrix products, arithmetic and copies ran while one was open for 1% of the time, Pallas kernels for 0%

profile of v1, /device:TPU:32, one launch (start us, length us, event | category | flops | bytes accessed | tf_op | source)
XLA Modules:
  0.0 628.5 jit_solution(16190913677927137950)
XLA Ops:
  9.6 7.3 %all-to-all-start = ((bf16[32,32,1024]{2,1,0:T(8,128)(2,1)}), bf16[32,32,1024]{2,1,0:T(8,128)(2,1)S(1)}, u32[]{:S(2)}, u32[]{:S(2)}) async-start(bf16[32,32,1024]{2,1,0:T(8,128)(2,1)} %stack.8), calls=%async_computation | async-start | bytes 4194304 | tf_op jit(solution)/shard_map/all_to_all | solution.py:91
  17.3 28.6 %all-to-all-done = bf16[32,32,1024]{2,1,0:T(8,128)(2,1)S(1)} async-done(((bf16[32,32,1024]{2,1,0:T(8,128)(2,1)}), bf16[32,32,1024]{2,1,0:T(8,128)(2,1)S(1)}, u32[]{:S(2)}, u32[]{:S(2)}) %all-to-all-start) | async-done | bytes 2097184 | tf_op jit(solution)/shard_map/all_to_all | solution.py:91
  45.9 3.1 fusion.2
  54.8 28.6 %all_gather.10 = f32[64,1024]{1,0:T(8,128)S(1)} all-gather(f32[64,128]{1,0:T(8,128)S(1)} %copy-done.11), channel_id=1, replica_groups=mesh['blk'=32,'row'=8] {'row'}, dimensions={1}, use_global_device_ids=true | all-gather | bytes 294912 | tf_op jit(solution)/shard_map/all_gather | solution.py:76
  86.0 16.9 %all-gather.2.cloned.1.call-done = bf16[8,32,8192]{2,0,1:T(8,128)(2,1)} async-done(((bf16[8,32,1024]{2,0,1:T(8,128)(2,1)}), bf16[8,32,8192]{2,0,1:T(8,128)(2,1)}) %all-gather.2.cloned.1.call-update) | async-done | bytes 4194320 | tf_op jit(solution)/shard_map/all_gather | solution.py:102
  102.9 21.7 %fusion.10 = (bf16[1,32,8192]{2,0,1:T(2,128)(2,1)S(1)}, bf16[1,32,8192]{2,0,1:T(2,128)(2,1)}, bf16[1,32,8192]{2,0,1:T(2,128)(2,1)}, bf16[1,32,8192]{2,0,1:T(2,12...) fusion(bf16[8,32,8192]{2,0,1:T(8,128)(2,1)} %all-gather.2.clone, ...), kind=kLoop, calls=%fused_computation.112 | loop fusion | bytes 8388608 | tf_op jit(solution)/shard_map/slice | solution.py:108
  127.8 31.4 %while.32 = (s32[]{:T(128)}, f32[128,1024]{1,0:T(8,128)S(1)}, bf16[32,8192]{1,0:T(8,128)(2,1)}, s32[]{:T(128)}, bf16[32,8192]{1,0:T(8,128)(2,1)S(1)}, /*index=5*...) while((s32[]{:T(128)}, f32[128,1024]{1,0:T(8,128)S(1)}, ...), condition=%wide.region_1.0_spmd.clone, body=%wide.region_0.0_spmd.clone.sunk | while | flops 542056448 | bytes 12533941 | solution.py:120
  127.8 3.0 multiply_convert_fusion.9
  131.8 3.8 convolution_add_fusion.4
  135.7 3.0 multiply_convert_fusion.9
  139.7 3.8 convolution_add_fusion.4
  143.5 3.0 multiply_convert_fusion.9
  147.5 3.8 convolution_add_fusion.4
  151.4 3.0 multiply_convert_fusion.9
  155.4 3.8 convolution_add_fusion.4
  159.2 6.7 %fusion.11 = (bf16[4,32,8192]{2,0,1:T(4,128)(2,1)S(1)}, bf16[4,32,8192]{2,0,1:T(4,128)(2,1)}) fusion(bf16[8,32,8192]{2,0,1:T(8,128)(2,1)} %all-gather.2.cloned.1.call-done), kind=kLoop, calls=%fused_computation.113 | loop fusion | bytes 8388608 | tf_op jit(solution)/shard_map/slice | solution.py:124
  179.4 3.6 copy_bitcast_fusion.2
  185.1 35.3 %while.33 = (s32[]{:T(128)}, f32[128,1024]{1,0:T(8,128)S(1)}, bf16[32,8192]{1,0:T(8,128)(2,1)}, s32[]{:T(128)}, bf16[32,8192]{1,0:T(8,128)(2,1)S(1)}, /*index=5*...) while((s32[]{:T(128)}, f32[128,1024]{1,0:T(8,128)S(1)}, ...), condition=%wide.region_3.0_spmd.clone, body=%wide.region_2.0_spmd.clone.sunk | while | flops 542056448 | bytes 12533941 | solution.py:120
  186.1 3.0 multiply_convert_fusion.11
  190.0 3.8 convolution_add_fusion.5
  194.9 3.0 multiply_convert_fusion.11
  198.8 3.8 convolution_add_fusion.5
  203.6 3.0 multiply_convert_fusion.11
  207.6 3.8 convolution_add_fusion.5
  216.4 3.8 convolution_add_fusion.5
  232.6 36.8 %reduce-scatter.3.cloned.1.call-done = f32[64,128]{0,1:T(8,128)} async-done(((f32[64,1024]{0,1:T(8,128)}), f32[64,128]{0,1:T(8,128)}) %reduce-scatter.3.cloned.1.call-update) | async-done | bytes 32784 | tf_op jit(solution)/shard_map/reduce_scatter | solution.py:133
  269.4 124.3 %psum.28 = f32[64,128]{0,1:T(8,128)S(1)} all-reduce(f32[64,128]{0,1:T(8,128)} %reduce-scatter.3.cloned.1.call-done), channel_id=1, replica_groups=mesh['blk'=32,'row'=8] {'blk'}, use_global_device_ids=true, to_apply=%region_13.0 | all-reduce | flops 8192 | bytes 65536 | tf_op jit(solution)/shard_map/psum | solution.py:134
  394.4 16.0 %psum.29 = f32[]{:T(128)} all-reduce(f32[]{:T(128)} %multiply_reduce_fusion.13), channel_id=1, replica_groups=mesh['blk'=32,'row'=8] {'row'}, use_global_device_ids=true, to_apply=%region_15.0 | all-reduce | flops 1 | bytes 8 | tf_op jit(solution)/shard_map/psum | solution.py:135
  411.2 24.3 %all_gather.11 = f32[64,1024]{0,1:T(8,128)S(1)} all-gather(f32[64,128]{0,1:T(8,128)S(1)} %multiply_add_fusion.1), channel_id=1, replica_groups=mesh['blk'=32,'row'=8] {'row'}, dimensions={1}, use_global_device_ids=true | all-gather | bytes 294912 | tf_op jit(solution)/shard_map/all_gather | solution.py:76
  444.6 34.0 %reduce-scatter.5.cloned.1.call-done = f32[64,128]{0,1:T(8,128)} async-done(((f32[64,1024]{0,1:T(8,128)}), f32[64,128]{0,1:T(8,128)}) %reduce-scatter.5.cloned.1.call-update) | async-done | bytes 32784 | tf_op jit(solution)/shard_map/reduce_scatter | solution.py:133
  478.6 124.3 %psum.30 = f32[64,128]{0,1:T(8,128)S(1)} all-reduce(f32[64,128]{0,1:T(8,128)} %reduce-scatter.5.cloned.1.call-done), channel_id=1, replica_groups=mesh['blk'=32,'row'=8] {'blk'}, use_global_device_ids=true, to_apply=%region_25.0 | all-reduce | flops 8192 | bytes 65536 | tf_op jit(solution)/shard_map/psum | solution.py:134
  604.6 15.9 %psum.31 = f32[]{:T(128)} all-reduce(f32[]{:T(128)} %multiply_reduce_fusion.8), channel_id=1, replica_groups=mesh['blk'=32,'row'=8] {'row'}, use_global_device_ids=true, to_apply=%region_27.0 | all-reduce | flops 1 | bytes 8 | tf_op jit(solution)/shard_map/psum | solution.py:135
  (159 shorter events, 63.5 us)
Async XLA Ops:
  7.2 9.9 %copy-start = (s32[64,4]{0,1:T(4,128)S(1)}, s32[64,4]{0,1:T(4,128)}, u32[]{:S(2)}) copy-start(s32[64,4]{0,1:T(4,128)} %param.8) | copy-start | bytes 3076
  9.6 36.3 %all-to-all-start = ((bf16[32,32,1024]{2,1,0:T(8,128)(2,1)}), bf16[32,32,1024]{2,1,0:T(8,128)(2,1)S(1)}, u32[]{:S(2)}, u32[]{:S(2)}) async-start(bf16[32,32,1024]{2,1,0:T(8,128)(2,1)} %stack.8), calls=%async_computation | async-start | bytes 4194304 | tf_op jit(solution)/shard_map/all_to_all | solution.py:91
  17.0 37.8 %copy-start.11 = (f32[64,128]{1,0:T(8,128)S(1)}, f32[64,128]{1,0:T(8,128)}, u32[]{:S(2)}) copy-start(f32[64,128]{1,0:T(8,128)} %param.9) | copy-start | bytes 98308
  17.0 86.0 %all-gather.2.cloned.1.call-start = ((), (), s32[]{:S(2)}) async-start(), calls=%async_computation.3 | async-start | bytes 4718592 | tf_op jit(solution)/shard_map/all_gather | solution.py:102
  49.0 220.4 %reduce-scatter.3.cloned.1.call-start = ((), (), s32[]{:S(2)}) async-start(), calls=%async_computation.4 | async-start | bytes 589824 | tf_op jit(solution)/shard_map/reduce_scatter | solution.py:133
  174.1 2.1 copy-start.12
  176.2 1.5 copy-start.2
  178.3 4.6 copy-start.4
  178.3 4.6 copy-start.6
  179.4 3.6 copy-start.7
  224.6 1.5 copy-start.1
  226.1 3.4 copy-start.3
  226.1 3.4 copy-start.5
  227.7 3.3 copy-start.10
  231.7 0.8 copy-start.9
  232.5 246.1 %reduce-scatter.5.cloned.1.call-start = ((), (), s32[]{:S(2)}) async-start(), calls=%async_computation.5 | async-start | bytes 589824 | tf_op jit(solution)/shard_map/reduce_scatter | solution.py:133
  443.8 0.8 copy-start.8
Sparse Core Ops, SparseCore 0:
  49.1 53.7 all-gather.1
  232.7 36.6 reduce-scatter.2
  444.7 33.8 reduce-scatter.4
